TPU v7x, 32 devices: a whole 2x2x4 slice. The times are simulated.
32 devices in a mesh: dp: 8 (over z, y), feat: 4 (over x, core).
Axes of the slice: x: 2, y: 2, z: 4, core: 2. Of those that a mesh axis runs over, the one named last changes fastest.
Arguments:
- activations: bfloat16 [16384, 2048], P('feat', 'dp'), may hold values from -6 to 6
- cotangent: bfloat16 [16384, 2048], P('feat', 'dp'), may hold values from -6 to 6
- r_mix: bfloat16 [64, 256, 256], P('feat', 'dp'), may hold values from -0.375 to 0.375
- l_mix: bfloat16 [256, 4096], P('feat', 'dp'), may hold values from -0.75 to 0.75
Outputs:
- grad_x: bfloat16 [16384, 2048], P('feat', 'dp')
- grad_r: float32 [64, 256, 256], P('feat', 'dp')
- grad_l: float32 [256, 4096], P('feat', 'dp')
All inputs are finite; a program needn't handle non-finite values.
Results may differ from a plain program's by a relative error of at most 0.0055.
Values may be sent and summed in bfloat16 or wider, within the bound.
No kernel may reach another device: no remote copies, remote signals or barrier semaphores. Data moves between devices by JAX's collectives and lax.ppermute only.
A program may use at most 64 MiB of HBM per device.

v0:
```python
import math
import jax
import jax.numpy as jnp
import numpy as np
from jax import lax
from jax.sharding import PartitionSpec as P

BLOCKS = 64
WIDTH = 256


def gelu_tanh(values):
    return jax.nn.gelu(values, approximate=True)


def slope_of(pre_act, upstream):
    _, pullback = jax.vjp(gelu_tanh, pre_act)
    return pullback(upstream.astype(jnp.float32))[0].astype(jnp.bfloat16)


def ring_of(mesh):
    row = mesh.devices[(slice(None),) + (0,) * (mesh.devices.ndim - 1)]
    size = len(row)
    try:
        spots = [tuple(d.coords) for d in row]
    except AttributeError:
        return list(range(size))
    near = [
        [j for j in range(size) if sum((abs(a - b) for a, b in zip(spots[i], spots[j]))) == 1]
        for i in range(size)
    ]
    path, seen, budget = ([0], {0}, [20000])

    def grow():
        budget[0] -= 1
        if budget[0] < 0:
            return False
        if len(path) == size:
            return 0 in near[path[-1]] or size <= 2
        here = path[-1]
        for nxt in sorted(near[here], key=lambda j: len([k for k in near[j] if k not in seen])):
            if nxt in seen:
                continue
            path.append(nxt)
            seen.add(nxt)
            if grow():
                return True
            path.pop()
            seen.discard(nxt)
        return False

    return list(path) if grow() else list(range(size))


def ring_reduce_scatter(parts, ring):
    n = len(ring)
    order = jnp.asarray(np.array(ring, np.int32))
    place = jnp.asarray(np.argsort(np.array(ring)).astype(np.int32))
    here = place[lax.axis_index("dp")]
    half = parts.shape[1] // 2
    halves = (parts[:, :half], parts[:, half:])
    forward = [(ring[p], ring[(p + 1) % n]) for p in range(n)]
    backward = [(ring[p], ring[(p - 1) % n]) for p in range(n)]
    totals = []
    for way, pairs, src in ((1, forward, halves[0]), (-1, backward, halves[1])):
        acc = None
        for step in range(n):
            owner = order[(here - way * (1 + step)) % n]
            mine = lax.dynamic_index_in_dim(src, owner, axis=0, keepdims=False)
            acc = mine if acc is None else acc + mine
            if step < n - 1:
                acc = lax.ppermute(acc, "dp", pairs)
        totals.append(acc)
    return jnp.concatenate(totals, axis=0)


def body(ring, activations, cotangent, r_mix, l_mix):
    tok_count = activations.shape[1]
    local_blocks = activations.shape[0] // WIDTH
    n_dp = lax.axis_size("dp")
    grad_scale = 1.0 / math.sqrt(tok_count * n_dp)
    x_blocks = activations.reshape(local_blocks, WIDTH, tok_count)
    g_blocks = cotangent.reshape(local_blocks, WIDTH, tok_count)
    g_cols = lax.all_to_all(g_blocks, "feat", split_axis=1, concat_axis=0, tiled=True)
    local_cols = l_mix.shape[0]
    rows_r = r_mix.shape[1]
    r_flat = r_mix.reshape(1, -1)
    packed = jnp.concatenate([r_flat, l_mix.reshape(1, -1)], axis=1)
    packed = lax.all_gather(packed, "dp", axis=0, tiled=True)
    r_size = r_flat.shape[1]
    r_whole = packed[:, :r_size].reshape(n_dp, local_blocks, rows_r, WIDTH)
    r_whole = jnp.transpose(r_whole, (1, 0, 2, 3)).reshape(local_blocks, n_dp * rows_r, WIDTH)
    l_whole = packed[:, r_size:].reshape(n_dp, local_cols, -1, BLOCKS)
    l_blocks = jnp.transpose(l_whole, (0, 2, 1, 3)).reshape(-1, local_cols, BLOCKS)
    mixed_rows = jnp.einsum(
        "bit,bio->bot", x_blocks, r_whole, preferred_element_type=jnp.float32
    ).astype(jnp.bfloat16)
    columns = lax.all_to_all(mixed_rows, "feat", split_axis=1, concat_axis=0, tiled=True)
    pre_act = jnp.einsum("bst,bsc->cst", columns, l_blocks, preferred_element_type=jnp.float32)
    slope_cols = slope_of(pre_act, g_cols)
    back_cols = jnp.einsum(
        "cst,bsc->sbt", slope_cols, l_blocks, preferred_element_type=jnp.float32
    ).astype(jnp.bfloat16)
    l_term = jnp.einsum("bst,cst->bsc", columns, slope_cols, preferred_element_type=jnp.float32)
    l_term = (l_term * grad_scale).reshape(n_dp, -1, local_cols, BLOCKS)
    grad_l = ring_reduce_scatter(l_term, ring)
    grad_l = jnp.transpose(grad_l, (1, 0, 2)).reshape(local_cols, -1)
    back_rows = lax.all_to_all(back_cols, "feat", split_axis=1, concat_axis=0, tiled=True)
    through_r = jnp.einsum("obt,bio->bit", back_rows, r_whole, preferred_element_type=jnp.float32)
    grad_x = (
        (g_blocks.astype(jnp.float32) + through_r)
        .astype(jnp.bfloat16)
        .reshape(local_blocks * WIDTH, tok_count)
    )
    r_term = (
        jnp.einsum("bit,obt->ibo", x_blocks, back_rows, preferred_element_type=jnp.float32)
        * grad_scale
    ).reshape(n_dp, rows_r, local_blocks, WIDTH)
    grad_r = ring_reduce_scatter(r_term, ring)
    grad_r = jnp.transpose(grad_r, (1, 0, 2))
    return (grad_x, grad_r, grad_l)


def solution(mesh):
    ring = ring_of(mesh)
    placed = (P("feat", "dp"), P("feat", "dp"), P("feat", "dp", None), P("feat", "dp"))
    return jax.shard_map(
        lambda *args: body(ring, *args),
        mesh=mesh,
        in_specs=placed,
        out_specs=(P("feat", "dp"), P("feat", "dp", None), P("feat", "dp")),
        check_vma=False,
    )
```

profile of v0, /device:TPU:0, one launch (start us, length us, event | category | flops | bytes accessed | tf_op | source)
XLA Modules:
  0.0 299.4 jit_solution(11265219353165768789)
XLA Ops:
  9.4 3.6 %maximum_bitcast_fusion = bf16[1,1,163840]{2,1,0:T(2,128)(2,1)} fusion(bf16[1,32768]{1,0:T(2,128)(2,1)S(1)} %bitcast.189, bf16[1,131072]{1,0:T(2,128)(2,1)S(1)} %reshape.111), kind=kLoop, calls=%fused_computation.22 | loop fusion | flops 655360 | bytes 655360
  13.0 4.1 %copy.37 = bf16[16,256,256]{2,0,1:T(8,128)(2,1)} copy(bf16[16,256,256]{2,1,0:T(8,128)(2,1)} %bitcast.183) | data formatting | bytes 4194304 | tf_op jit(solution)/shard_map/reshape | solution.py:83
  17.1 4.5 %all-to-all-start = ((bf16[16,256,256]{2,0,1:T(8,128)(2,1)}), bf16[16,256,256]{2,0,1:T(8,128)(2,1)}, u32[]{:S(2)}, u32[]{:S(2)}) async-start(bf16[16,256,256]{2,0,1:T(8,128)(2,1)} %copy.37), calls=%async_computation | async-start | bytes 4194304 | tf_op jit(solution)/shard_map/all_to_all | solution.py:84
  21.6 80.6 %all-gather.3.cloned.1.call-done = bf16[8,1,163840]{2,1,0:T(2,128)(2,1)} async-done(((bf16[1,1,163840]{2,1,0:T(2,128)(2,1)}), bf16[8,1,163840]{2,1,0:T(2,128)(2,1)}) %all-gather.3.cloned.1.call-update) | async-done | bytes 2621456 | tf_op jit(solution)/shard_map/all_gather | solution.py:89
  102.1 5.8 %copy.58 = bf16[8,1,163840]{2,0,1:T(8,128)(2,1)S(1)} copy(bf16[8,1,163840]{2,1,0:T(2,128)(2,1)} %all-gather.3.cloned.1.call-done) | data formatting | bytes 5242880
  111.5 2.5 copy.40
  114.0 4.8 %all-to-all-start.1 = ((bf16[16,256,256]{2,0,1:T(8,128)(2,1)}), bf16[16,256,256]{2,0,1:T(8,128)(2,1)}, u32[]{:S(2)}, u32[]{:S(2)}) async-start(bf16[16,256,256]{2,0,1:T(8,128)(2,1)} %copy.40), calls=%async_computation.1 | async-start | bytes 4194304 | tf_op jit(solution)/shard_map/all_to_all | solution.py:98
  160.8 4.2 %copy.38 = f32[16,4,64,256]{3,0,1,2:T(8,128)} copy(bf16[16,4,64,256]{3,0,2,1:T(8,128)(2,1)} %bitcast.92) | data formatting | bytes 6291456 | tf_op jit(solution)/shard_map/convert_element_type | solution.py:18
  166.0 2.1 reshape.115
  169.6 2.0 copy.41
  172.4 5.1 %fusion.6 = bf16[64,64,256]{2,0,1:T(8,128)(2,1)S(1)} fusion(f32[16,4,64,256]{3,0,1,2:T(8,128)S(1)} %copy-done.6, bf16[64,64,256]{2,0,1:T(8,128)(2,1)S(1)} %bitcast.179, bf16[64,64,64]{2,1,0:T(8,128)(2,1)S(1)} %bitcast.185), kind=kOutput, calls=%fused_computation.8 | convolution fusion | flops 155189248 | bytes 8912896 | tf_op jit(solution)/shard_map/bst,bsc->cst/dot_general | solution.py:99
  177.5 2.0 multiply_bitcast_fusion
  180.8 2.5 copy.44
  183.4 3.8 %copy.46 = f32[64,64,64]{2,1,0:T(8,128)} copy(f32[64,64,64]{0,2,1:T(8,128)} %multiply_bitcast_fusion) | data formatting | bytes 2097152 | tf_op jit(solution)/shard_map/mul | solution.py:105
  187.2 2.7 fusion.13
  189.9 4.5 %all-to-all-start.2 = ((bf16[64,64,256]{2,0,1:T(8,128)(2,1)}), bf16[64,64,256]{2,0,1:T(8,128)(2,1)}, u32[]{:S(2)}, u32[]{:S(2)}) async-start(bf16[64,64,256]{2,0,1:T(8,128)(2,1)} %copy.44), calls=%async_computation.2 | async-start | bytes 4194304 | tf_op jit(solution)/shard_map/all_to_all | solution.py:108
  197.4 3.8 %collective-permute-done.21 = f32[4,64,64]{2,1,0:T(8,128)S(1)} collective-permute-done((f32[4,64,64]{2,1,0:T(8,128)S(1)}, f32[4,64,64]{2,1,0:T(8,128)S(1)}, u32[]{:S(2)}, u32[]{:S(2)}) %collective-permute-start.21) | collective-permute-done | bytes 65568 | tf_op jit(solution)/shard_map/ppermute | solution.py:72
  204.3 3.1 %collective-permute-done.22 = f32[4,64,64]{2,1,0:T(8,128)S(1)} collective-permute-done((f32[4,64,64]{2,1,0:T(8,128)S(1)}, f32[4,64,64]{2,1,0:T(8,128)S(1)}, u32[]{:S(2)}, u32[]{:S(2)}) %collective-permute-start.22) | collective-permute-done | bytes 65568 | tf_op jit(solution)/shard_map/ppermute | solution.py:72
  210.4 2.9 collective-permute-done.23
  216.4 2.9 collective-permute-done.24
  222.3 2.9 collective-permute-done.25
  235.2 2.4 collective-permute-done.7
  237.7 2.6 collective-permute-start.8
  241.4 2.1 collective-permute-start.27
  243.5 3.2 %collective-permute-done.8 = f32[16,16,256]{2,0,1:T(8,128)S(1)} collective-permute-done((f32[16,16,256]{2,0,1:T(8,128)S(1)}, f32[16,16,256]{2,0,1:T(8,128)S(1)}, u32[]{:S(2)}, u32[]{:S(2)}) %collective-permute-start.8) | collective-permute-done | bytes 262176 | tf_op jit(solution)/shard_map/ppermute | solution.py:72
  246.8 2.5 collective-permute-start.9
  251.0 4.7 %collective-permute-done.9 = f32[16,16,256]{2,0,1:T(8,128)S(1)} collective-permute-done((f32[16,16,256]{2,0,1:T(8,128)S(1)}, f32[16,16,256]{2,0,1:T(8,128)S(1)}, u32[]{:S(2)}, u32[]{:S(2)}) %collective-permute-start.9) | collective-permute-done | bytes 262176 | tf_op jit(solution)/shard_map/ppermute | solution.py:72
  255.8 2.5 collective-permute-start.10
  259.4 5.3 %collective-permute-done.10 = f32[16,16,256]{2,0,1:T(8,128)S(1)} collective-permute-done((f32[16,16,256]{2,0,1:T(8,128)S(1)}, f32[16,16,256]{2,0,1:T(8,128)S(1)}, u32[]{:S(2)}, u32[]{:S(2)}) %collective-permute-start.10) | collective-permute-done | bytes 262176 | tf_op jit(solution)/shard_map/ppermute | solution.py:72
  266.9 5.8 %collective-permute-done.11 = f32[16,16,256]{2,0,1:T(8,128)S(1)} collective-permute-done((f32[16,16,256]{2,0,1:T(8,128)S(1)}, f32[16,16,256]{2,0,1:T(8,128)S(1)}, u32[]{:S(2)}, u32[]{:S(2)}) %collective-permute-start.11) | collective-permute-done | bytes 262176 | tf_op jit(solution)/shard_map/ppermute | solution.py:72
  275.9 4.9 %collective-permute-done.12 = f32[16,16,256]{2,0,1:T(8,128)S(1)} collective-permute-done((f32[16,16,256]{2,0,1:T(8,128)S(1)}, f32[16,16,256]{2,0,1:T(8,128)S(1)}, u32[]{:S(2)}, u32[]{:S(2)}) %collective-permute-start.12) | collective-permute-done | bytes 262176 | tf_op jit(solution)/shard_map/ppermute | solution.py:72
  284.9 4.9 %add_convert_fusion = bf16[16,256,256]{2,1,0:T(8,128)(2,1)} fusion(bf16[16,256,256]{2,1,0:T(8,128)(2,1)} %bitcast.184, bf16[16,256,256]{2,1,0:T(8,128)(2,1)} %bitcast.173, bf16[256,16,256]{2,0,1:T(8,128)(2,1)} %bitcast.175), kind=kOutput, calls=%fused_computation.14 | convolution fusion | flops 540016640 | bytes 8388608 | tf_op jit(solution)/shard_map/obt,bio->bit/dot_general | solution.py:109
  (113 shorter events, 53.3 us)
Async XLA Ops:
  7.2 94.9 %all-gather.3.cloned.1.call-start = ((), (), s32[]{:S(2)}) async-start(), calls=%async_computation.3 | async-start | bytes 5898240 | tf_op jit(solution)/shard_map/all_gather | solution.py:89
  17.1 96.9 %all-to-all-start = ((bf16[16,256,256]{2,0,1:T(8,128)(2,1)}), bf16[16,256,256]{2,0,1:T(8,128)(2,1)}, u32[]{:S(2)}, u32[]{:S(2)}) async-start(bf16[16,256,256]{2,0,1:T(8,128)(2,1)} %copy.37), calls=%async_computation | async-start | bytes 4194304 | tf_op jit(solution)/shard_map/all_to_all | solution.py:84
  114.0 55.6 %all-to-all-start.1 = ((bf16[16,256,256]{2,0,1:T(8,128)(2,1)}), bf16[16,256,256]{2,0,1:T(8,128)(2,1)}, u32[]{:S(2)}, u32[]{:S(2)}) async-start(bf16[16,256,256]{2,0,1:T(8,128)(2,1)} %copy.40), calls=%async_computation.1 | async-start | bytes 4194304 | tf_op jit(solution)/shard_map/all_to_all | solution.py:98
  189.9 36.7 %all-to-all-start.2 = ((bf16[64,64,256]{2,0,1:T(8,128)(2,1)}), bf16[64,64,256]{2,0,1:T(8,128)(2,1)}, u32[]{:S(2)}, u32[]{:S(2)}) async-start(bf16[64,64,256]{2,0,1:T(8,128)(2,1)} %copy.44), calls=%async_computation.2 | async-start | bytes 4194304 | tf_op jit(solution)/shard_map/all_to_all | solution.py:108
  195.3 5.9 %collective-permute-start.21 = (f32[4,64,64]{2,1,0:T(8,128)S(1)}, f32[4,64,64]{2,1,0:T(8,128)S(1)}, u32[]{:S(2)}, u32[]{:S(2)}) collective-permute-start(f32[4,64,64]{2,1,0:T(8,128)S(1)} %dynamic-slice_bitcast_fusion.2), channel_id=1, source_target_pairs={{0,8},{4,0},{12,4},{20,12},{28,20},{24,28},{16,24},{8,16},{1,9},{5... | collective-permute-start | bytes 196616 | tf_op jit(solution)/shard_map/ppermute | solution.py:72
  195.7 6.8 %collective-permute-start.14 = (f32[4,64,64]{2,1,0:T(8,128)S(1)}, f32[4,64,64]{2,1,0:T(8,128)S(1)}, u32[]{:S(2)}, u32[]{:S(2)}) collective-permute-start(f32[4,64,64]{2,1,0:T(8,128)S(1)} %dynamic-slice_bitcast_fusion.3), channel_id=1, source_target_pairs={{0,4},{4,12},{12,20},{20,28},{28,24},{24,16},{16,8},{8,0},{1,5},{5... | collective-permute-start | bytes 196616 | tf_op jit(solution)/shard_map/ppermute | solution.py:72
  202.1 5.2 %collective-permute-start.22 = (f32[4,64,64]{2,1,0:T(8,128)S(1)}, f32[4,64,64]{2,1,0:T(8,128)S(1)}, u32[]{:S(2)}, u32[]{:S(2)}) collective-permute-start(f32[4,64,64]{2,1,0:T(8,128)S(1)} %bitcast_add_fusion.20), channel_id=1, source_target_pairs={{0,8},{4,0},{12,4},{20,12},{28,20},{24,28},{16,24},{8,16},{1,9},{5... | collective-permute-start | bytes 196616 | tf_op jit(solution)/shard_map/ppermute | solution.py:72
  202.6 6.1 %collective-permute-start.15 = (f32[4,64,64]{2,1,0:T(8,128)S(1)}, f32[4,64,64]{2,1,0:T(8,128)S(1)}, u32[]{:S(2)}, u32[]{:S(2)}) collective-permute-start(f32[4,64,64]{2,1,0:T(8,128)S(1)} %bitcast_add_fusion.27), channel_id=1, source_target_pairs={{0,4},{4,12},{12,20},{20,28},{28,24},{24,16},{16,8},{8,0},{1,5},{5... | collective-permute-start | bytes 196616 | tf_op jit(solution)/shard_map/ppermute | solution.py:72
  208.3 5.0 %collective-permute-start.23 = (f32[4,64,64]{2,1,0:T(8,128)S(1)}, f32[4,64,64]{2,1,0:T(8,128)S(1)}, u32[]{:S(2)}, u32[]{:S(2)}) collective-permute-start(f32[4,64,64]{2,1,0:T(8,128)S(1)} %bitcast_add_fusion.19), channel_id=1, source_target_pairs={{0,8},{4,0},{12,4},{20,12},{28,20},{24,28},{16,24},{8,16},{1,9},{5... | collective-permute-start | bytes 196616 | tf_op jit(solution)/shard_map/ppermute | solution.py:72
  208.7 5.9 %collective-permute-start.16 = (f32[4,64,64]{2,1,0:T(8,128)S(1)}, f32[4,64,64]{2,1,0:T(8,128)S(1)}, u32[]{:S(2)}, u32[]{:S(2)}) collective-permute-start(f32[4,64,64]{2,1,0:T(8,128)S(1)} %bitcast_add_fusion.26), channel_id=1, source_target_pairs={{0,4},{4,12},{12,20},{20,28},{28,24},{24,16},{16,8},{8,0},{1,5},{5... | collective-permute-start | bytes 196616 | tf_op jit(solution)/shard_map/ppermute | solution.py:72
  214.2 5.0 %collective-permute-start.24 = (f32[4,64,64]{2,1,0:T(8,128)S(1)}, f32[4,64,64]{2,1,0:T(8,128)S(1)}, u32[]{:S(2)}, u32[]{:S(2)}) collective-permute-start(f32[4,64,64]{2,1,0:T(8,128)S(1)} %bitcast_add_fusion.18), channel_id=1, source_target_pairs={{0,8},{4,0},{12,4},{20,12},{28,20},{24,28},{16,24},{8,16},{1,9},{5... | collective-permute-start | bytes 196616 | tf_op jit(solution)/shard_map/ppermute | solution.py:72
  214.7 5.9 %collective-permute-start.17 = (f32[4,64,64]{2,1,0:T(8,128)S(1)}, f32[4,64,64]{2,1,0:T(8,128)S(1)}, u32[]{:S(2)}, u32[]{:S(2)}) collective-permute-start(f32[4,64,64]{2,1,0:T(8,128)S(1)} %bitcast_add_fusion.25), channel_id=1, source_target_pairs={{0,4},{4,12},{12,20},{20,28},{28,24},{24,16},{16,8},{8,0},{1,5},{5... | collective-permute-start | bytes 196616 | tf_op jit(solution)/shard_map/ppermute | solution.py:72
  220.1 5.1 %collective-permute-start.25 = (f32[4,64,64]{2,1,0:T(8,128)S(1)}, f32[4,64,64]{2,1,0:T(8,128)S(1)}, u32[]{:S(2)}, u32[]{:S(2)}) collective-permute-start(f32[4,64,64]{2,1,0:T(8,128)S(1)} %bitcast_add_fusion.17), channel_id=1, source_target_pairs={{0,8},{4,0},{12,4},{20,12},{28,20},{24,28},{16,24},{8,16},{1,9},{5... | collective-permute-start | bytes 196616 | tf_op jit(solution)/shard_map/ppermute | solution.py:72
  220.6 12.0 %collective-permute-start.18 = (f32[4,64,64]{2,1,0:T(8,128)S(1)}, f32[4,64,64]{2,1,0:T(8,128)}, u32[]{:S(2)}, u32[]{:S(2)}) collective-permute-start(f32[4,64,64]{2,1,0:T(8,128)S(1)} %bitcast_add_fusion.24), channel_id=1, source_target_pairs={{0,4},{4,12},{12,20},{20,28},{28,24},{24,16},{16,8},{8,0},{1,5},{5... | collective-permute-start | bytes 196616 | tf_op jit(solution)/shard_map/ppermute | solution.py:72
  226.1 14.3 %collective-permute-start.26 = (f32[4,64,64]{2,1,0:T(8,128)S(1)}, f32[4,64,64]{2,1,0:T(8,128)S(1)}, u32[]{:S(2)}, u32[]{:S(2)}) collective-permute-start(f32[4,64,64]{2,1,0:T(8,128)S(1)} %bitcast_add_fusion.16), channel_id=1, source_target_pairs={{0,8},{4,0},{12,4},{20,12},{28,20},{24,28},{16,24},{8,16},{1,9},{5... | collective-permute-start | bytes 196616 | tf_op jit(solution)/shard_map/ppermute | solution.py:72
  230.5 7.2 %collective-permute-start.7 = (f32[16,16,256]{2,0,1:T(8,128)S(1)}, f32[16,16,256]{2,0,1:T(8,128)S(1)}, u32[]{:S(2)}, u32[]{:S(2)}) collective-permute-start(f32[16,16,256]{2,0,1:T(8,128)S(1)} %dynamic-slice_bitcast_fusion), channel_id=1, source_target_pairs={{0,8},{4,0},{12,4},{20,12},{28,20},{24,28},{16,24},{8,16},{1,9},{5... | collective-permute-start | bytes 786440 | tf_op jit(solution)/shard_map/ppermute | solution.py:72
  232.2 8.2 %collective-permute-start = (f32[16,16,256]{2,0,1:T(8,128)S(1)}, f32[16,16,256]{2,0,1:T(8,128)S(1)}, u32[]{:S(2)}, u32[]{:S(2)}) collective-permute-start(f32[16,16,256]{2,0,1:T(8,128)S(1)} %dynamic-slice_bitcast_fusion.1), channel_id=1, source_target_pairs={{0,4},{4,12},{12,20},{20,28},{28,24},{24,16},{16,8},{8,0},{1,5},{5... | collective-permute-start | bytes 786440 | tf_op jit(solution)/shard_map/ppermute | solution.py:72
  233.5 15.9 %collective-permute-start.19 = (f32[4,64,64]{2,1,0:T(8,128)S(1)}, f32[4,64,64]{2,1,0:T(8,128)S(1)}, u32[]{:S(2)}, u32[]{:S(2)}) collective-permute-start(f32[4,64,64]{2,1,0:T(8,128)S(1)} %bitcast_add_fusion.23), channel_id=1, source_target_pairs={{0,4},{4,12},{12,20},{20,28},{28,24},{24,16},{16,8},{8,0},{1,5},{5... | collective-permute-start | bytes 196616 | tf_op jit(solution)/shard_map/ppermute | solution.py:72
  237.7 9.0 %collective-permute-start.8 = (f32[16,16,256]{2,0,1:T(8,128)S(1)}, f32[16,16,256]{2,0,1:T(8,128)S(1)}, u32[]{:S(2)}, u32[]{:S(2)}) collective-permute-start(f32[16,16,256]{2,0,1:T(8,128)S(1)} %bitcast_add_fusion.6), channel_id=1, source_target_pairs={{0,8},{4,0},{12,4},{20,12},{28,20},{24,28},{16,24},{8,16},{1,9},{5... | collective-permute-start | bytes 786440 | tf_op jit(solution)/shard_map/ppermute | solution.py:72
  240.4 8.9 %collective-permute-start.1 = (f32[16,16,256]{2,0,1:T(8,128)S(1)}, f32[16,16,256]{2,0,1:T(8,128)S(1)}, u32[]{:S(2)}, u32[]{:S(2)}) collective-permute-start(f32[16,16,256]{2,0,1:T(8,128)S(1)} %bitcast_add_fusion.13), channel_id=1, source_target_pairs={{0,4},{4,12},{12,20},{20,28},{28,24},{24,16},{16,8},{8,0},{1,5},{5... | collective-permute-start | bytes 786440 | tf_op jit(solution)/shard_map/ppermute | solution.py:72
  241.4 17.0 %collective-permute-start.27 = (f32[4,64,64]{2,1,0:T(8,128)S(1)}, f32[4,64,64]{2,1,0:T(8,128)S(1)}, u32[]{:S(2)}, u32[]{:S(2)}) collective-permute-start(f32[4,64,64]{2,1,0:T(8,128)S(1)} %bitcast_add_fusion.15), channel_id=1, source_target_pairs={{0,8},{4,0},{12,4},{20,12},{28,20},{24,28},{16,24},{8,16},{1,9},{5... | collective-permute-start | bytes 196616 | tf_op jit(solution)/shard_map/ppermute | solution.py:72
  246.8 9.0 %collective-permute-start.9 = (f32[16,16,256]{2,0,1:T(8,128)S(1)}, f32[16,16,256]{2,0,1:T(8,128)S(1)}, u32[]{:S(2)}, u32[]{:S(2)}) collective-permute-start(f32[16,16,256]{2,0,1:T(8,128)S(1)} %bitcast_add_fusion.5), channel_id=1, source_target_pairs={{0,8},{4,0},{12,4},{20,12},{28,20},{24,28},{16,24},{8,16},{1,9},{5... | collective-permute-start | bytes 786440 | tf_op jit(solution)/shard_map/ppermute | solution.py:72
  249.3 9.0 %collective-permute-start.2 = (f32[16,16,256]{2,0,1:T(8,128)S(1)}, f32[16,16,256]{2,0,1:T(8,128)S(1)}, u32[]{:S(2)}, u32[]{:S(2)}) collective-permute-start(f32[16,16,256]{2,0,1:T(8,128)S(1)} %bitcast_add_fusion.12), channel_id=1, source_target_pairs={{0,4},{4,12},{12,20},{20,28},{28,24},{24,16},{16,8},{8,0},{1,5},{5... | collective-permute-start | bytes 786440 | tf_op jit(solution)/shard_map/ppermute | solution.py:72
  249.4 17.5 %collective-permute-start.20 = (f32[4,64,64]{2,1,0:T(8,128)S(1)}, f32[4,64,64]{2,1,0:T(8,128)S(1)}, u32[]{:S(2)}, u32[]{:S(2)}) collective-permute-start(f32[4,64,64]{2,1,0:T(8,128)S(1)} %bitcast_add_fusion.22), channel_id=1, source_target_pairs={{0,4},{4,12},{12,20},{20,28},{28,24},{24,16},{16,8},{8,0},{1,5},{5... | collective-permute-start | bytes 196616 | tf_op jit(solution)/shard_map/ppermute | solution.py:72
  255.8 8.9 %collective-permute-start.10 = (f32[16,16,256]{2,0,1:T(8,128)S(1)}, f32[16,16,256]{2,0,1:T(8,128)S(1)}, u32[]{:S(2)}, u32[]{:S(2)}) collective-permute-start(f32[16,16,256]{2,0,1:T(8,128)S(1)} %bitcast_add_fusion.4), channel_id=1, source_target_pairs={{0,8},{4,0},{12,4},{20,12},{28,20},{24,28},{16,24},{8,16},{1,9},{5... | collective-permute-start | bytes 786440 | tf_op jit(solution)/shard_map/ppermute | solution.py:72
  258.3 8.1 %collective-permute-start.3 = (f32[16,16,256]{2,0,1:T(8,128)S(1)}, f32[16,16,256]{2,0,1:T(8,128)S(1)}, u32[]{:S(2)}, u32[]{:S(2)}) collective-permute-start(f32[16,16,256]{2,0,1:T(8,128)S(1)} %bitcast_add_fusion.11), channel_id=1, source_target_pairs={{0,4},{4,12},{12,20},{20,28},{28,24},{24,16},{16,8},{8,0},{1,5},{5... | collective-permute-start | bytes 786440 | tf_op jit(solution)/shard_map/ppermute | solution.py:72
  264.7 8.0 %collective-permute-start.11 = (f32[16,16,256]{2,0,1:T(8,128)S(1)}, f32[16,16,256]{2,0,1:T(8,128)S(1)}, u32[]{:S(2)}, u32[]{:S(2)}) collective-permute-start(f32[16,16,256]{2,0,1:T(8,128)S(1)} %bitcast_add_fusion.3), channel_id=1, source_target_pairs={{0,8},{4,0},{12,4},{20,12},{28,20},{24,28},{16,24},{8,16},{1,9},{5... | collective-permute-start | bytes 786440 | tf_op jit(solution)/shard_map/ppermute | solution.py:72
  266.5 7.3 %collective-permute-start.4 = (f32[16,16,256]{2,0,1:T(8,128)S(1)}, f32[16,16,256]{2,0,1:T(8,128)S(1)}, u32[]{:S(2)}, u32[]{:S(2)}) collective-permute-start(f32[16,16,256]{2,0,1:T(8,128)S(1)} %bitcast_add_fusion.10), channel_id=1, source_target_pairs={{0,4},{4,12},{12,20},{20,28},{28,24},{24,16},{16,8},{8,0},{1,5},{5... | collective-permute-start | bytes 786440 | tf_op jit(solution)/shard_map/ppermute | solution.py:72
  272.7 8.0 %collective-permute-start.12 = (f32[16,16,256]{2,0,1:T(8,128)S(1)}, f32[16,16,256]{2,0,1:T(8,128)S(1)}, u32[]{:S(2)}, u32[]{:S(2)}) collective-permute-start(f32[16,16,256]{2,0,1:T(8,128)S(1)} %bitcast_add_fusion.2), channel_id=1, source_target_pairs={{0,8},{4,0},{12,4},{20,12},{28,20},{24,28},{16,24},{8,16},{1,9},{5... | collective-permute-start | bytes 786440 | tf_op jit(solution)/shard_map/ppermute | solution.py:72
  273.8 8.3 %collective-permute-start.5 = (f32[16,16,256]{2,0,1:T(8,128)S(1)}, f32[16,16,256]{2,0,1:T(8,128)S(1)}, u32[]{:S(2)}, u32[]{:S(2)}) collective-permute-start(f32[16,16,256]{2,0,1:T(8,128)S(1)} %bitcast_add_fusion.9), channel_id=1, source_target_pairs={{0,4},{4,12},{12,20},{20,28},{28,24},{24,16},{16,8},{8,0},{1,5},{5... | collective-permute-start | bytes 786440 | tf_op jit(solution)/shard_map/ppermute | solution.py:72
  281.7 8.0 %collective-permute-start.13 = (f32[16,16,256]{2,0,1:T(8,128)S(1)}, f32[16,16,256]{2,0,1:T(8,128)S(1)}, u32[]{:S(2)}, u32[]{:S(2)}) collective-permute-start(f32[16,16,256]{2,0,1:T(8,128)S(1)} %bitcast_add_fusion.1), channel_id=1, source_target_pairs={{0,8},{4,0},{12,4},{20,12},{28,20},{24,28},{16,24},{8,16},{1,9},{5... | collective-permute-start | bytes 786440 | tf_op jit(solution)/shard_map/ppermute | solution.py:72
  283.1 7.7 %collective-permute-start.6 = (f32[16,16,256]{2,0,1:T(8,128)S(1)}, f32[16,16,256]{2,0,1:T(8,128)S(1)}, u32[]{:S(2)}, u32[]{:S(2)}) collective-permute-start(f32[16,16,256]{2,0,1:T(8,128)S(1)} %bitcast_add_fusion.8), channel_id=1, source_target_pairs={{0,4},{4,12},{12,20},{20,28},{28,24},{24,16},{16,8},{8,0},{1,5},{5... | collective-permute-start | bytes 786440 | tf_op jit(solution)/shard_map/ppermute | solution.py:72
  (9 other events, 216.5 us)
Sparse Core Ops, SparseCore 0:
  13.1 88.9 all-gather.2
where the time goes:
time: 301 us; the launch traced here: 299 us
  waiting for transfers between devices  122 us (41%)
  between operations  55.1 us (18%)
  starting transfers between devices  46.6 us (15%)
  local copies, waits for them, and re-layouts  44.2 us (15%)
  other arithmetic  16.3 us (5%)
  matrix products  14.8 us (5%)
    all_gather x1, waiting for transfers between devices, body(): packed = lax.all_gather(packed, 'dp', axis=0, tiled=True)  80.6 us
    ppermute x28, waiting for transfers between devices, ring_reduce_scatter(): acc = lax.ppermute(acc, 'dp', pairs)  41.8 us
    ppermute x28, starting transfers between devices, ring_reduce_scatter(): acc = lax.ppermute(acc, 'dp', pairs)  32.9 us
    add x28, other arithmetic, ring_reduce_scatter(): acc = mine if acc is None else acc + mine  11.8 us
    unnamed x20, local copies, waits for them, and re-layouts  10.3 us
  transfers between devices with their start and end apart: 32, of which 13 were waited for; matrix products, arithmetic and copies ran while one was open for 15% of the time, Pallas kernels for 0%

commit v1 on v0

--- a/solution.py
+++ b/solution.py
@@ -95,7 +95,12 @@
     mixed_rows = jnp.einsum(
         "bit,bio->bot", x_blocks, r_whole, preferred_element_type=jnp.float32
     ).astype(jnp.bfloat16)
-    columns = lax.all_to_all(mixed_rows, "feat", split_axis=1, concat_axis=0, tiled=True)
+    columns = jnp.concatenate(
+        lax.all_to_all(
+            jnp.stack(jnp.split(mixed_rows, lax.axis_size("feat"), axis=1)), "feat", 0, 0
+        ),
+        axis=0,
+    )
     pre_act = jnp.einsum("bst,bsc->cst", columns, l_blocks, preferred_element_type=jnp.float32)
     slope_cols = slope_of(pre_act, g_cols)
     back_cols = jnp.einsum(

time: 301 us -> 302 us (level)
  local copies, waits for them, and re-layouts: 44.2 us -> 39.1 us
  matrix products: 14.8 us -> 19.2 us
    unnamed x20 -> x18, local copies, waits for them, and re-layouts: 10.3 us -> 9.49 us
where the time goes in v1:
time: 302 us; the launch traced here: 300 us
  waiting for transfers between devices  123 us (41%)
  between operations  55 us (18%)
  starting transfers between devices  46.6 us (15%)
  local copies, waits for them, and re-layouts  39.1 us (13%)
  matrix products  19.2 us (6%)
  other arithmetic  17.9 us (6%)
    all_gather x1, waiting for transfers between devices, body(): packed = lax.all_gather(packed, 'dp', axis=0, tiled=True)  80.6 us
    ppermute x28, waiting for transfers between devices, ring_reduce_scatter(): acc = lax.ppermute(acc, 'dp', pairs)  42 us
    ppermute x28, starting transfers between devices, ring_reduce_scatter(): acc = lax.ppermute(acc, 'dp', pairs)  32.9 us
    add x28, other arithmetic, ring_reduce_scatter(): acc = mine if acc is None else acc + mine  11.8 us
    unnamed x18, local copies, waits for them, and re-layouts  9.49 us
    dot_general x1, matrix products, body(): jnp.einsum('bst,bsc->cst', columns, l_blocks, preferred_element_type=jnp....  7 us
  transfers between devices with their start and end apart: 32, of which 13 were waited for; matrix products, arithmetic and copies ran while one was open for 15% of the time, Pallas kernels for 0%

profile of v1, /device:TPU:0, one launch (start us, length us, event | category | flops | bytes accessed | tf_op | source)
XLA Modules:
  0.0 300.3 jit_solution(3507732845981775973)
XLA Ops:
  9.4 3.6 %maximum_bitcast_fusion = bf16[1,1,163840]{2,1,0:T(2,128)(2,1)} fusion(bf16[1,32768]{1,0:T(2,128)(2,1)S(1)} %bitcast.190, bf16[1,131072]{1,0:T(2,128)(2,1)S(1)} %reshape.114), kind=kLoop, calls=%fused_computation.26 | loop fusion | flops 655360 | bytes 655360
  13.0 4.1 %copy.40 = bf16[16,256,256]{2,0,1:T(8,128)(2,1)} copy(bf16[16,256,256]{2,1,0:T(8,128)(2,1)} %bitcast.184) | data formatting | bytes 4194304 | tf_op jit(solution)/shard_map/reshape | solution.py:83
  17.1 4.5 %all-to-all-start = ((bf16[16,256,256]{2,0,1:T(8,128)(2,1)}), bf16[16,256,256]{2,0,1:T(8,128)(2,1)}, u32[]{:S(2)}, u32[]{:S(2)}) async-start(bf16[16,256,256]{2,0,1:T(8,128)(2,1)} %copy.40), calls=%async_computation | async-start | bytes 4194304 | tf_op jit(solution)/shard_map/all_to_all | solution.py:84
  21.6 80.6 %all-gather.3.cloned.1.call-done = bf16[8,1,163840]{2,1,0:T(2,128)(2,1)} async-done(((bf16[1,1,163840]{2,1,0:T(2,128)(2,1)}), bf16[8,1,163840]{2,1,0:T(2,128)(2,1)}) %all-gather.3.cloned.1.call-update) | async-done | bytes 2621456 | tf_op jit(solution)/shard_map/all_gather | solution.py:89
  102.1 5.8 %copy.67 = bf16[8,1,163840]{2,0,1:T(8,128)(2,1)S(1)} copy(bf16[8,1,163840]{2,1,0:T(2,128)(2,1)} %all-gather.3.cloned.1.call-done) | data formatting | bytes 5242880
  113.2 4.8 %all-to-all-start.1 = ((bf16[4,16,64,256]{3,2,1,0:T(8,128)(2,1)}), bf16[4,16,64,256]{3,2,1,0:T(8,128)(2,1)}, u32[]{:S(2)}, u32[]{:S(2)}) async-start(bf16[4,16,64,256]{3,2,1,0:T(8,128)(2,1)} %pad_maximum_fusion), calls=%async_computation.1 | async-start | bytes 4194304 | tf_op jit(solution)/shard_map/all_to_all | solution.py:99
  160.0 4.2 %copy.41 = f32[16,4,64,256]{3,0,1,2:T(8,128)} copy(bf16[16,4,64,256]{3,0,2,1:T(8,128)(2,1)} %bitcast.93) | data formatting | bytes 6291456 | tf_op jit(solution)/shard_map/convert_element_type | solution.py:18
  165.2 2.1 reshape.118
  168.8 7.0 %fusion.6 = bf16[64,64,256]{2,0,1:T(8,128)(2,1)S(1)} fusion(f32[16,4,64,256]{3,0,1,2:T(8,128)} %copy.41, bf16[64,64,256]{2,1,0:T(8,128)(2,1)} %bitcast.14, bf16[64,64,64]{2,1,0:T(8,128)(2,1)S(1)} %bitcast.186), kind=kOutput, calls=%fused_computation.8 | convolution fusion | flops 155189248 | bytes 8912896 | tf_op jit(solution)/shard_map/bst,bsc->cst/dot_general | solution.py:104
  175.8 4.5 %multiply_bitcast_fusion = f32[64,64,64]{0,2,1:T(8,128)} fusion(bf16[64,64,256]{2,0,1:T(8,128)(2,1)S(1)} %fusion.6, bf16[64,64,256]{2,1,0:T(8,128)(2,1)} %bitcast.14), kind=kOutput, calls=%fused_computation.18 | convolution fusion | flops 134479872 | bytes 5242880 | tf_op jit(solution)/shard_map/bst,cst->bsc/dot_general | solution.py:109
  181.6 2.5 copy.46
  184.1 3.8 %copy.49 = f32[64,64,64]{2,1,0:T(8,128)} copy(f32[64,64,64]{0,2,1:T(8,128)} %multiply_bitcast_fusion) | data formatting | bytes 2097152 | tf_op jit(solution)/shard_map/mul | solution.py:110
  187.9 2.7 fusion.18
  190.6 4.5 %all-to-all-start.2 = ((bf16[64,64,256]{2,0,1:T(8,128)(2,1)}), bf16[64,64,256]{2,0,1:T(8,128)(2,1)}, u32[]{:S(2)}, u32[]{:S(2)}) async-start(bf16[64,64,256]{2,0,1:T(8,128)(2,1)} %copy.46), calls=%async_computation.2 | async-start | bytes 4194304 | tf_op jit(solution)/shard_map/all_to_all | solution.py:113
  198.2 3.8 %collective-permute-done.21 = f32[4,64,64]{2,1,0:T(8,128)S(1)} collective-permute-done((f32[4,64,64]{2,1,0:T(8,128)S(1)}, f32[4,64,64]{2,1,0:T(8,128)S(1)}, u32[]{:S(2)}, u32[]{:S(2)}) %collective-permute-start.21) | collective-permute-done | bytes 65568 | tf_op jit(solution)/shard_map/ppermute | solution.py:72
  205.0 3.1 %collective-permute-done.22 = f32[4,64,64]{2,1,0:T(8,128)S(1)} collective-permute-done((f32[4,64,64]{2,1,0:T(8,128)S(1)}, f32[4,64,64]{2,1,0:T(8,128)S(1)}, u32[]{:S(2)}, u32[]{:S(2)}) %collective-permute-start.22) | collective-permute-done | bytes 65568 | tf_op jit(solution)/shard_map/ppermute | solution.py:72
  211.2 2.9 collective-permute-done.23
  217.3 2.9 collective-permute-done.24
  223.3 2.9 collective-permute-done.25
  227.6 1.8 copy.47
  236.2 2.6 collective-permute-done.7
  238.9 2.4 collective-permute-start.8
  242.6 2.1 collective-permute-start.27
  244.7 3.1 %collective-permute-done.8 = f32[16,16,256]{2,0,1:T(8,128)S(1)} collective-permute-done((f32[16,16,256]{2,0,1:T(8,128)S(1)}, f32[16,16,256]{2,0,1:T(8,128)S(1)}, u32[]{:S(2)}, u32[]{:S(2)}) %collective-permute-start.8) | collective-permute-done | bytes 262176 | tf_op jit(solution)/shard_map/ppermute | solution.py:72
  247.8 2.5 collective-permute-start.9
  252.1 4.6 %collective-permute-done.9 = f32[16,16,256]{2,0,1:T(8,128)S(1)} collective-permute-done((f32[16,16,256]{2,0,1:T(8,128)S(1)}, f32[16,16,256]{2,0,1:T(8,128)S(1)}, u32[]{:S(2)}, u32[]{:S(2)}) %collective-permute-start.9) | collective-permute-done | bytes 262176 | tf_op jit(solution)/shard_map/ppermute | solution.py:72
  256.8 2.5 collective-permute-start.10
  260.4 5.4 %collective-permute-done.10 = f32[16,16,256]{2,0,1:T(8,128)S(1)} collective-permute-done((f32[16,16,256]{2,0,1:T(8,128)S(1)}, f32[16,16,256]{2,0,1:T(8,128)S(1)}, u32[]{:S(2)}, u32[]{:S(2)}) %collective-permute-start.10) | collective-permute-done | bytes 262176 | tf_op jit(solution)/shard_map/ppermute | solution.py:72
  268.0 5.7 %collective-permute-done.11 = f32[16,16,256]{2,0,1:T(8,128)S(1)} collective-permute-done((f32[16,16,256]{2,0,1:T(8,128)S(1)}, f32[16,16,256]{2,0,1:T(8,128)S(1)}, u32[]{:S(2)}, u32[]{:S(2)}) %collective-permute-start.11) | collective-permute-done | bytes 262176 | tf_op jit(solution)/shard_map/ppermute | solution.py:72
  276.8 4.8 %collective-permute-done.12 = f32[16,16,256]{2,0,1:T(8,128)S(1)} collective-permute-done((f32[16,16,256]{2,0,1:T(8,128)S(1)}, f32[16,16,256]{2,0,1:T(8,128)S(1)}, u32[]{:S(2)}, u32[]{:S(2)}) %collective-permute-start.12) | collective-permute-done | bytes 262176 | tf_op jit(solution)/shard_map/ppermute | solution.py:72
  284.0 1.8 collective-permute-start.6
  285.8 4.9 %add_convert_fusion = bf16[16,256,256]{2,1,0:T(8,128)(2,1)} fusion(bf16[16,256,256]{2,1,0:T(8,128)(2,1)} %bitcast.185, bf16[16,256,256]{2,1,0:T(8,128)(2,1)} %bitcast.176, bf16[256,16,256]{2,0,1:T(8,128)(2,1)} %bitcast.178), kind=kOutput, calls=%fused_computation.14 | convolution fusion | flops 540016640 | bytes 8388608 | tf_op jit(solution)/shard_map/obt,bio->bit/dot_general | solution.py:114
  (111 shorter events, 51.0 us)
Async XLA Ops:
  7.2 94.9 %all-gather.3.cloned.1.call-start = ((), (), s32[]{:S(2)}) async-start(), calls=%async_computation.3 | async-start | bytes 5898240 | tf_op jit(solution)/shard_map/all_gather | solution.py:89
  17.1 96.1 %all-to-all-start = ((bf16[16,256,256]{2,0,1:T(8,128)(2,1)}), bf16[16,256,256]{2,0,1:T(8,128)(2,1)}, u32[]{:S(2)}, u32[]{:S(2)}) async-start(bf16[16,256,256]{2,0,1:T(8,128)(2,1)} %copy.40), calls=%async_computation | async-start | bytes 4194304 | tf_op jit(solution)/shard_map/all_to_all | solution.py:84
  113.2 55.6 %all-to-all-start.1 = ((bf16[4,16,64,256]{3,2,1,0:T(8,128)(2,1)}), bf16[4,16,64,256]{3,2,1,0:T(8,128)(2,1)}, u32[]{:S(2)}, u32[]{:S(2)}) async-start(bf16[4,16,64,256]{3,2,1,0:T(8,128)(2,1)} %pad_maximum_fusion), calls=%async_computation.1 | async-start | bytes 4194304 | tf_op jit(solution)/shard_map/all_to_all | solution.py:99
  190.6 36.9 %all-to-all-start.2 = ((bf16[64,64,256]{2,0,1:T(8,128)(2,1)}), bf16[64,64,256]{2,0,1:T(8,128)(2,1)}, u32[]{:S(2)}, u32[]{:S(2)}) async-start(bf16[64,64,256]{2,0,1:T(8,128)(2,1)} %copy.46), calls=%async_computation.2 | async-start | bytes 4194304 | tf_op jit(solution)/shard_map/all_to_all | solution.py:113
  196.0 5.9 %collective-permute-start.21 = (f32[4,64,64]{2,1,0:T(8,128)S(1)}, f32[4,64,64]{2,1,0:T(8,128)S(1)}, u32[]{:S(2)}, u32[]{:S(2)}) collective-permute-start(f32[4,64,64]{2,1,0:T(8,128)S(1)} %dynamic-slice_bitcast_fusion.2), channel_id=1, source_target_pairs={{0,8},{4,0},{12,4},{20,12},{28,20},{24,28},{16,24},{8,16},{1,9},{5... | collective-permute-start | bytes 196616 | tf_op jit(solution)/shard_map/ppermute | solution.py:72
  196.5 6.8 %collective-permute-start.14 = (f32[4,64,64]{2,1,0:T(8,128)S(1)}, f32[4,64,64]{2,1,0:T(8,128)S(1)}, u32[]{:S(2)}, u32[]{:S(2)}) collective-permute-start(f32[4,64,64]{2,1,0:T(8,128)S(1)} %dynamic-slice_bitcast_fusion.3), channel_id=1, source_target_pairs={{0,4},{4,12},{12,20},{20,28},{28,24},{24,16},{16,8},{8,0},{1,5},{5... | collective-permute-start | bytes 196616 | tf_op jit(solution)/shard_map/ppermute | solution.py:72
  202.9 5.2 %collective-permute-start.22 = (f32[4,64,64]{2,1,0:T(8,128)S(1)}, f32[4,64,64]{2,1,0:T(8,128)S(1)}, u32[]{:S(2)}, u32[]{:S(2)}) collective-permute-start(f32[4,64,64]{2,1,0:T(8,128)S(1)} %bitcast_add_fusion.20), channel_id=1, source_target_pairs={{0,8},{4,0},{12,4},{20,12},{28,20},{24,28},{16,24},{8,16},{1,9},{5... | collective-permute-start | bytes 196616 | tf_op jit(solution)/shard_map/ppermute | solution.py:72
  203.3 6.1 %collective-permute-start.15 = (f32[4,64,64]{2,1,0:T(8,128)S(1)}, f32[4,64,64]{2,1,0:T(8,128)S(1)}, u32[]{:S(2)}, u32[]{:S(2)}) collective-permute-start(f32[4,64,64]{2,1,0:T(8,128)S(1)} %bitcast_add_fusion.27), channel_id=1, source_target_pairs={{0,4},{4,12},{12,20},{20,28},{28,24},{24,16},{16,8},{8,0},{1,5},{5... | collective-permute-start | bytes 196616 | tf_op jit(solution)/shard_map/ppermute | solution.py:72
  209.0 5.0 %collective-permute-start.23 = (f32[4,64,64]{2,1,0:T(8,128)S(1)}, f32[4,64,64]{2,1,0:T(8,128)S(1)}, u32[]{:S(2)}, u32[]{:S(2)}) collective-permute-start(f32[4,64,64]{2,1,0:T(8,128)S(1)} %bitcast_add_fusion.19), channel_id=1, source_target_pairs={{0,8},{4,0},{12,4},{20,12},{28,20},{24,28},{16,24},{8,16},{1,9},{5... | collective-permute-start | bytes 196616 | tf_op jit(solution)/shard_map/ppermute | solution.py:72
  209.5 6.1 %collective-permute-start.16 = (f32[4,64,64]{2,1,0:T(8,128)S(1)}, f32[4,64,64]{2,1,0:T(8,128)S(1)}, u32[]{:S(2)}, u32[]{:S(2)}) collective-permute-start(f32[4,64,64]{2,1,0:T(8,128)S(1)} %bitcast_add_fusion.26), channel_id=1, source_target_pairs={{0,4},{4,12},{12,20},{20,28},{28,24},{24,16},{16,8},{8,0},{1,5},{5... | collective-permute-start | bytes 196616 | tf_op jit(solution)/shard_map/ppermute | solution.py:72
  215.0 5.2 %collective-permute-start.24 = (f32[4,64,64]{2,1,0:T(8,128)S(1)}, f32[4,64,64]{2,1,0:T(8,128)S(1)}, u32[]{:S(2)}, u32[]{:S(2)}) collective-permute-start(f32[4,64,64]{2,1,0:T(8,128)S(1)} %bitcast_add_fusion.18), channel_id=1, source_target_pairs={{0,8},{4,0},{12,4},{20,12},{28,20},{24,28},{16,24},{8,16},{1,9},{5... | collective-permute-start | bytes 196616 | tf_op jit(solution)/shard_map/ppermute | solution.py:72
  215.7 5.9 %collective-permute-start.17 = (f32[4,64,64]{2,1,0:T(8,128)S(1)}, f32[4,64,64]{2,1,0:T(8,128)S(1)}, u32[]{:S(2)}, u32[]{:S(2)}) collective-permute-start(f32[4,64,64]{2,1,0:T(8,128)S(1)} %bitcast_add_fusion.25), channel_id=1, source_target_pairs={{0,4},{4,12},{12,20},{20,28},{28,24},{24,16},{16,8},{8,0},{1,5},{5... | collective-permute-start | bytes 196616 | tf_op jit(solution)/shard_map/ppermute | solution.py:72
  221.1 5.1 %collective-permute-start.25 = (f32[4,64,64]{2,1,0:T(8,128)S(1)}, f32[4,64,64]{2,1,0:T(8,128)S(1)}, u32[]{:S(2)}, u32[]{:S(2)}) collective-permute-start(f32[4,64,64]{2,1,0:T(8,128)S(1)} %bitcast_add_fusion.17), channel_id=1, source_target_pairs={{0,8},{4,0},{12,4},{20,12},{28,20},{24,28},{16,24},{8,16},{1,9},{5... | collective-permute-start | bytes 196616 | tf_op jit(solution)/shard_map/ppermute | solution.py:72
  221.6 12.0 %collective-permute-start.18 = (f32[4,64,64]{2,1,0:T(8,128)S(1)}, f32[4,64,64]{2,1,0:T(8,128)}, u32[]{:S(2)}, u32[]{:S(2)}) collective-permute-start(f32[4,64,64]{2,1,0:T(8,128)S(1)} %bitcast_add_fusion.24), channel_id=1, source_target_pairs={{0,4},{4,12},{12,20},{20,28},{28,24},{24,16},{16,8},{8,0},{1,5},{5... | collective-permute-start | bytes 196616 | tf_op jit(solution)/shard_map/ppermute | solution.py:72
  227.1 14.6 %collective-permute-start.26 = (f32[4,64,64]{2,1,0:T(8,128)S(1)}, f32[4,64,64]{2,1,0:T(8,128)S(1)}, u32[]{:S(2)}, u32[]{:S(2)}) collective-permute-start(f32[4,64,64]{2,1,0:T(8,128)S(1)} %bitcast_add_fusion.16), channel_id=1, source_target_pairs={{0,8},{4,0},{12,4},{20,12},{28,20},{24,28},{16,24},{8,16},{1,9},{5... | collective-permute-start | bytes 196616 | tf_op jit(solution)/shard_map/ppermute | solution.py:72
  231.4 7.4 %collective-permute-start.7 = (f32[16,16,256]{2,0,1:T(8,128)S(1)}, f32[16,16,256]{2,0,1:T(8,128)S(1)}, u32[]{:S(2)}, u32[]{:S(2)}) collective-permute-start(f32[16,16,256]{2,0,1:T(8,128)S(1)} %dynamic-slice_bitcast_fusion), channel_id=1, source_target_pairs={{0,8},{4,0},{12,4},{20,12},{28,20},{24,28},{16,24},{8,16},{1,9},{5... | collective-permute-start | bytes 786440 | tf_op jit(solution)/shard_map/ppermute | solution.py:72
  233.2 8.4 %collective-permute-start = (f32[16,16,256]{2,0,1:T(8,128)S(1)}, f32[16,16,256]{2,0,1:T(8,128)S(1)}, u32[]{:S(2)}, u32[]{:S(2)}) collective-permute-start(f32[16,16,256]{2,0,1:T(8,128)S(1)} %dynamic-slice_bitcast_fusion.1), channel_id=1, source_target_pairs={{0,4},{4,12},{12,20},{20,28},{28,24},{24,16},{16,8},{8,0},{1,5},{5... | collective-permute-start | bytes 786440 | tf_op jit(solution)/shard_map/ppermute | solution.py:72
  234.5 15.9 %collective-permute-start.19 = (f32[4,64,64]{2,1,0:T(8,128)S(1)}, f32[4,64,64]{2,1,0:T(8,128)S(1)}, u32[]{:S(2)}, u32[]{:S(2)}) collective-permute-start(f32[4,64,64]{2,1,0:T(8,128)S(1)} %bitcast_add_fusion.23), channel_id=1, source_target_pairs={{0,4},{4,12},{12,20},{20,28},{28,24},{24,16},{16,8},{8,0},{1,5},{5... | collective-permute-start | bytes 196616 | tf_op jit(solution)/shard_map/ppermute | solution.py:72
  238.9 8.9 %collective-permute-start.8 = (f32[16,16,256]{2,0,1:T(8,128)S(1)}, f32[16,16,256]{2,0,1:T(8,128)S(1)}, u32[]{:S(2)}, u32[]{:S(2)}) collective-permute-start(f32[16,16,256]{2,0,1:T(8,128)S(1)} %bitcast_add_fusion.6), channel_id=1, source_target_pairs={{0,8},{4,0},{12,4},{20,12},{28,20},{24,28},{16,24},{8,16},{1,9},{5... | collective-permute-start | bytes 786440 | tf_op jit(solution)/shard_map/ppermute | solution.py:72
  241.6 8.7 %collective-permute-start.1 = (f32[16,16,256]{2,0,1:T(8,128)S(1)}, f32[16,16,256]{2,0,1:T(8,128)S(1)}, u32[]{:S(2)}, u32[]{:S(2)}) collective-permute-start(f32[16,16,256]{2,0,1:T(8,128)S(1)} %bitcast_add_fusion.13), channel_id=1, source_target_pairs={{0,4},{4,12},{12,20},{20,28},{28,24},{24,16},{16,8},{8,0},{1,5},{5... | collective-permute-start | bytes 786440 | tf_op jit(solution)/shard_map/ppermute | solution.py:72
  242.6 16.8 %collective-permute-start.27 = (f32[4,64,64]{2,1,0:T(8,128)S(1)}, f32[4,64,64]{2,1,0:T(8,128)S(1)}, u32[]{:S(2)}, u32[]{:S(2)}) collective-permute-start(f32[4,64,64]{2,1,0:T(8,128)S(1)} %bitcast_add_fusion.15), channel_id=1, source_target_pairs={{0,8},{4,0},{12,4},{20,12},{28,20},{24,28},{16,24},{8,16},{1,9},{5... | collective-permute-start | bytes 196616 | tf_op jit(solution)/shard_map/ppermute | solution.py:72
  247.8 8.9 %collective-permute-start.9 = (f32[16,16,256]{2,0,1:T(8,128)S(1)}, f32[16,16,256]{2,0,1:T(8,128)S(1)}, u32[]{:S(2)}, u32[]{:S(2)}) collective-permute-start(f32[16,16,256]{2,0,1:T(8,128)S(1)} %bitcast_add_fusion.5), channel_id=1, source_target_pairs={{0,8},{4,0},{12,4},{20,12},{28,20},{24,28},{16,24},{8,16},{1,9},{5... | collective-permute-start | bytes 786440 | tf_op jit(solution)/shard_map/ppermute | solution.py:72
  250.4 8.9 %collective-permute-start.2 = (f32[16,16,256]{2,0,1:T(8,128)S(1)}, f32[16,16,256]{2,0,1:T(8,128)S(1)}, u32[]{:S(2)}, u32[]{:S(2)}) collective-permute-start(f32[16,16,256]{2,0,1:T(8,128)S(1)} %bitcast_add_fusion.12), channel_id=1, source_target_pairs={{0,4},{4,12},{12,20},{20,28},{28,24},{24,16},{16,8},{8,0},{1,5},{5... | collective-permute-start | bytes 786440 | tf_op jit(solution)/shard_map/ppermute | solution.py:72
  250.5 17.5 %collective-permute-start.20 = (f32[4,64,64]{2,1,0:T(8,128)S(1)}, f32[4,64,64]{2,1,0:T(8,128)S(1)}, u32[]{:S(2)}, u32[]{:S(2)}) collective-permute-start(f32[4,64,64]{2,1,0:T(8,128)S(1)} %bitcast_add_fusion.22), channel_id=1, source_target_pairs={{0,4},{4,12},{12,20},{20,28},{28,24},{24,16},{16,8},{8,0},{1,5},{5... | collective-permute-start | bytes 196616 | tf_op jit(solution)/shard_map/ppermute | solution.py:72
  256.8 9.0 %collective-permute-start.10 = (f32[16,16,256]{2,0,1:T(8,128)S(1)}, f32[16,16,256]{2,0,1:T(8,128)S(1)}, u32[]{:S(2)}, u32[]{:S(2)}) collective-permute-start(f32[16,16,256]{2,0,1:T(8,128)S(1)} %bitcast_add_fusion.4), channel_id=1, source_target_pairs={{0,8},{4,0},{12,4},{20,12},{28,20},{24,28},{16,24},{8,16},{1,9},{5... | collective-permute-start | bytes 786440 | tf_op jit(solution)/shard_map/ppermute | solution.py:72
  259.3 8.1 %collective-permute-start.3 = (f32[16,16,256]{2,0,1:T(8,128)S(1)}, f32[16,16,256]{2,0,1:T(8,128)S(1)}, u32[]{:S(2)}, u32[]{:S(2)}) collective-permute-start(f32[16,16,256]{2,0,1:T(8,128)S(1)} %bitcast_add_fusion.11), channel_id=1, source_target_pairs={{0,4},{4,12},{12,20},{20,28},{28,24},{24,16},{16,8},{8,0},{1,5},{5... | collective-permute-start | bytes 786440 | tf_op jit(solution)/shard_map/ppermute | solution.py:72
  265.8 7.9 %collective-permute-start.11 = (f32[16,16,256]{2,0,1:T(8,128)S(1)}, f32[16,16,256]{2,0,1:T(8,128)S(1)}, u32[]{:S(2)}, u32[]{:S(2)}) collective-permute-start(f32[16,16,256]{2,0,1:T(8,128)S(1)} %bitcast_add_fusion.3), channel_id=1, source_target_pairs={{0,8},{4,0},{12,4},{20,12},{28,20},{24,28},{16,24},{8,16},{1,9},{5... | collective-permute-start | bytes 786440 | tf_op jit(solution)/shard_map/ppermute | solution.py:72
  267.4 7.2 %collective-permute-start.4 = (f32[16,16,256]{2,0,1:T(8,128)S(1)}, f32[16,16,256]{2,0,1:T(8,128)S(1)}, u32[]{:S(2)}, u32[]{:S(2)}) collective-permute-start(f32[16,16,256]{2,0,1:T(8,128)S(1)} %bitcast_add_fusion.10), channel_id=1, source_target_pairs={{0,4},{4,12},{12,20},{20,28},{28,24},{24,16},{16,8},{8,0},{1,5},{5... | collective-permute-start | bytes 786440 | tf_op jit(solution)/shard_map/ppermute | solution.py:72
  273.7 7.9 %collective-permute-start.12 = (f32[16,16,256]{2,0,1:T(8,128)S(1)}, f32[16,16,256]{2,0,1:T(8,128)S(1)}, u32[]{:S(2)}, u32[]{:S(2)}) collective-permute-start(f32[16,16,256]{2,0,1:T(8,128)S(1)} %bitcast_add_fusion.2), channel_id=1, source_target_pairs={{0,8},{4,0},{12,4},{20,12},{28,20},{24,28},{16,24},{8,16},{1,9},{5... | collective-permute-start | bytes 786440 | tf_op jit(solution)/shard_map/ppermute | solution.py:72
  274.7 8.3 %collective-permute-start.5 = (f32[16,16,256]{2,0,1:T(8,128)S(1)}, f32[16,16,256]{2,0,1:T(8,128)S(1)}, u32[]{:S(2)}, u32[]{:S(2)}) collective-permute-start(f32[16,16,256]{2,0,1:T(8,128)S(1)} %bitcast_add_fusion.9), channel_id=1, source_target_pairs={{0,4},{4,12},{12,20},{20,28},{28,24},{24,16},{16,8},{8,0},{1,5},{5... | collective-permute-start | bytes 786440 | tf_op jit(solution)/shard_map/ppermute | solution.py:72
  282.6 8.0 %collective-permute-start.13 = (f32[16,16,256]{2,0,1:T(8,128)S(1)}, f32[16,16,256]{2,0,1:T(8,128)S(1)}, u32[]{:S(2)}, u32[]{:S(2)}) collective-permute-start(f32[16,16,256]{2,0,1:T(8,128)S(1)} %bitcast_add_fusion.1), channel_id=1, source_target_pairs={{0,8},{4,0},{12,4},{20,12},{28,20},{24,28},{16,24},{8,16},{1,9},{5... | collective-permute-start | bytes 786440 | tf_op jit(solution)/shard_map/ppermute | solution.py:72
  284.0 7.7 %collective-permute-start.6 = (f32[16,16,256]{2,0,1:T(8,128)S(1)}, f32[16,16,256]{2,0,1:T(8,128)S(1)}, u32[]{:S(2)}, u32[]{:S(2)}) collective-permute-start(f32[16,16,256]{2,0,1:T(8,128)S(1)} %bitcast_add_fusion.8), channel_id=1, source_target_pairs={{0,4},{4,12},{12,20},{20,28},{28,24},{24,16},{16,8},{8,0},{1,5},{5... | collective-permute-start | bytes 786440 | tf_op jit(solution)/shard_map/ppermute | solution.py:72
  (8 other events, 213.6 us)
Sparse Core Ops, SparseCore 0:
  13.1 88.9 all-gather.2
